TPU v7x, 512 devices: a whole 4x4x16 slice. The times are simulated.
512 devices in a mesh: section: 8 (over z_hi, core), tp: 64 (over x, z_lo, y).
Axes of the slice: x: 4, y: 4, z: 16 (z_hi: 4, z_lo: 4; z = z_hi * 4 + z_lo), core: 2. Of those that a mesh axis runs over, the one named last changes fastest.
Arguments:
- incoming: bfloat16 [8, 320, 8192], P('section', None, 'tp'), may hold values from -6 to 6
- norm_gain: bfloat16 [8, 8192], P('section', 'tp'), may hold values from 0.5 to 1.5
- query_weight: bfloat16 [8, 8192, 8192], P('section', 'tp'), may hold values from -0.0625 to 0.0625
- query_scale: float32 [8, 64, 64], P('section', 'tp'), may hold values from 0.3 to 3
- query_keep: int32 [8, 64, 64], P('section', 'tp'), may hold values from 0 to 1, as said below
- kv_weight: bfloat16 [8, 8192, 2048], P('section', 'tp'), may hold values from -0.0625 to 0.0625
- kv_scale: float32 [8, 64, 16], P('section', 'tp'), may hold values from 0.3 to 3
- kv_keep: int32 [8, 64, 16], P('section', 'tp'), may hold values from 0 to 1, as said below
- out_weight: bfloat16 [8, 8192, 8192], P('section', 'tp'), may hold values from -0.0625 to 0.0625
- out_scale: float32 [8, 64, 64], P('section', 'tp'), may hold values from 0.3 to 3
- out_keep: int32 [8, 64, 64], P('section', 'tp'), may hold values from 0 to 1, as said below
- documents: int32 [320], replicated, may hold values from 0 to 3, never falling along the last dimension, each value on 1 to 160 neighbouring positions
Outputs:
- passed: bfloat16 [8, 320, 8192], P('section', None, 'tp')
Inputs may be any that keep to these rules, and one draw needn't show every extreme that they name: `documents`: document numbers never fall along the tokens; every document has 1 to 160 tokens and one has exactly 160. `query_keep`: 1 keeps the block, 0 removes it. `kv_keep`: 1 keeps the block, 0 removes it. `out_keep`: 1 keeps the block, 0 removes it.
All inputs are finite; a program needn't handle non-finite values.
Results may differ from a plain program's by a relative error of at most 0.006.
Values may be sent and summed in bfloat16 or wider, within the bound.
No kernel may reach another device: no remote copies, remote signals or barrier semaphores. Data moves between devices by JAX's collectives and lax.ppermute only.
A program may use at most 64 MiB of HBM per device.

v0:
```python
import jax
import jax.numpy as jnp
from jax import lax
from jax.sharding import PartitionSpec as P

D = 8192
HEADS = 64
KV_HEADS = 8
HD = 128
BLK = 128
rope_base = 500000.0
epsilon = 1e-05


def passed_along(value, axis, steps):
    count = lax.axis_size(axis)
    pairs = [(source, (source + steps) % count) for source in range(count)]
    return lax.ppermute(value, axis, pairs)


def dequant(weight, scale, keep):
    row_count, col_count = weight.shape
    factor = scale * keep.astype(jnp.float32)
    blocks = weight.astype(jnp.float32).reshape(row_count // BLK, BLK, col_count // BLK, BLK)
    blocks = blocks * factor[:, None, :, None]
    return blocks.reshape(row_count, col_count).astype(jnp.bfloat16)


def rotate(values, first_col):
    row_count, col_count = values.shape
    columns = first_col + 2 * jnp.arange(col_count // 2, dtype=jnp.int32)
    frequency = rope_base ** (-(columns % HD).astype(jnp.float32) / HD)
    angles = jnp.arange(row_count, dtype=jnp.float32)[:, None] * frequency[None, :]
    paired = values.reshape(row_count, col_count // 2, 2)
    even_part = paired[:, :, 0]
    odd_part = paired[:, :, 1]
    cosine = jnp.cos(angles)
    sine = jnp.sin(angles)
    turned = jnp.stack(
        (even_part * cosine - odd_part * sine, even_part * sine + odd_part * cosine), axis=-1
    )
    return turned.reshape(row_count, col_count)


def rotate_keys(values, first_col, kv_width):
    col_ids = first_col + jnp.arange(values.shape[1], dtype=jnp.int32)
    return jnp.where(col_ids[None, :] < kv_width, rotate(values, first_col), values)


def local(
    incoming,
    norm_gain,
    query_weight,
    query_scale,
    query_keep,
    kv_weight,
    kv_scale,
    kv_keep,
    out_weight,
    out_scale,
    out_keep,
    documents,
):
    own_index = lax.axis_index("tp")
    local_rows = incoming[0]
    tok_count, own_width = local_rows.shape
    activ = local_rows.astype(jnp.float32)
    kv_width = KV_HEADS * HD
    group_size = HEADS // KV_HEADS
    partial_value = jnp.sum(activ * activ, axis=1, keepdims=True)
    squares = lax.psum(partial_value, "tp")
    normed = (activ * lax.rsqrt(squares / D + epsilon) * norm_gain[0].astype(jnp.float32)).astype(
        jnp.bfloat16
    )
    normed_all = lax.all_gather(normed, "tp", axis=1, tiled=True)
    q_eff = dequant(query_weight[0], query_scale[0], query_keep[0])
    q_columns = lax.all_to_all(q_eff, "tp", split_axis=1, concat_axis=0, tiled=True)
    q_width = q_columns.shape[1]
    queries = jnp.dot(normed_all, q_columns, preferred_element_type=jnp.float32)
    queries = rotate(queries, own_index * q_width).astype(jnp.bfloat16)
    kv_eff = dequant(kv_weight[0], kv_scale[0], kv_keep[0])
    kv_total = lax.psum(jnp.dot(normed, kv_eff, preferred_element_type=jnp.float32), "tp")
    keyval = rotate_keys(kv_total, 0, kv_width).astype(jnp.bfloat16)
    heads_here = q_width // HD
    kv_index = own_index * heads_here // group_size
    key_rows = lax.dynamic_slice_in_dim(keyval, kv_index * HD, HD, 1)
    value_rows = lax.dynamic_slice_in_dim(keyval, kv_width + kv_index * HD, HD, 1)
    token_ids = jnp.arange(tok_count, dtype=jnp.int32)
    allowed = (documents[:, None] == documents[None, :]) & (
        token_ids[:, None] >= token_ids[None, :]
    )
    query_three = queries.reshape(tok_count, heads_here, HD)
    scores = jnp.einsum(
        "thd,sd->hts", query_three, key_rows, preferred_element_type=jnp.float32
    ) / jnp.sqrt(jnp.float32(HD))
    exp_scores = jnp.where(allowed[None], jnp.exp(scores), jnp.float32(0.0))
    probs = (exp_scores / jnp.sum(exp_scores, axis=-1, keepdims=True)).astype(jnp.bfloat16)
    head_out = jnp.einsum("hts,sd->thd", probs, value_rows, preferred_element_type=jnp.float32)
    head_out = head_out.astype(jnp.bfloat16).reshape(tok_count, q_width)
    o_eff = dequant(out_weight[0], out_scale[0], out_keep[0])
    o_columns = lax.all_to_all(o_eff, "tp", split_axis=1, concat_axis=0, tiled=True)
    mixed_sum = jnp.dot(
        lax.all_gather(head_out, "tp", axis=1, tiled=True),
        o_columns,
        preferred_element_type=jnp.float32,
    )
    layer_out = (activ + mixed_sum).astype(jnp.bfloat16)
    received = passed_along(layer_out, "section", 1)
    return received[None]


def solution(mesh):
    placed = (
        P("section", None, "tp"),
        P("section", "tp"),
        P("section", "tp", None),
        P("section", "tp", None),
        P("section", "tp", None),
        P("section", "tp", None),
        P("section", "tp", None),
        P("section", "tp", None),
        P("section", "tp", None),
        P("section", "tp", None),
        P("section", "tp", None),
        P(),
    )
    return jax.shard_map(
        local, mesh=mesh, in_specs=placed, out_specs=P("section", None, "tp"), check_vma=False
    )
```

profile of v0, /device:TPU:1, one launch (start us, length us, event | category | flops | bytes accessed | tf_op | source)
XLA Modules:
  0.0 1547.2 jit_solution(16440638860779838320)
XLA Ops:
  7.6 163.6 %psum.14 = f32[320,1]{0,1:T(1,128)S(1)} all-reduce(f32[320,1]{0,1:T(1,128)S(1)} %broadcast_in_dim.16), channel_id=1, replica_groups=mesh['section'=8,'tp'=64] {'tp'}, use_global_device_ids=true, to_apply=%region_1.0 | all-reduce | flops 320 | bytes 2560 | tf_op jit(solution)/shard_map/psum | solution.py:71
  172.6 3.2 fusion.20
  177.4 3.2 copy.32
  182.5 5.6 all-to-all-start
  188.2 699.4 %all-reduce.2.cloned.1.call-done = f32[320,2048]{1,0:T(8,128)} async-done(((f32[320,2048]{1,0:T(8,128)}), f32[320,2048]{1,0:T(8,128)}) %all-reduce.2.cloned.1.call-update) | async-done | bytes 2621456 | tf_op jit(solution)/shard_map/psum | solution.py:82
  887.7 3.5 copy.27
  891.2 3.7 reshape.383
  894.9 4.1 fusion.55
  899.0 3.7 copy.39
  902.7 3.5 copy.40
  906.2 7.1 multiply_subtract_fusion
  918.0 2.7 copy.31
  920.7 2.8 select_convert_fusion
  923.5 3.2 copy.33
  926.7 2.9 copy.34
  929.6 3.2 dot_general.21
  932.8 255.4 %all-gather.4.cloned.1.call-done = bf16[320,8192]{1,0:T(8,128)(2,1)} async-done(((bf16[320,128]{1,0:T(8,128)(2,1)}), bf16[320,8192]{1,0:T(8,128)(2,1)}) %all-gather.4.cloned.1.call-update) | async-done | bytes 5242896 | tf_op jit(solution)/shard_map/all_gather | solution.py:75
  1188.2 5.1 fusion.2
  1197.0 3.4 copy.37
  1201.0 37.8 %all_to_all.32 = bf16[128,64,128]{0,2,1:T(8,128)(2,1)S(1)} all-to-all(bf16[128,64,128]{0,2,1:T(8,128)(2,1)S(1)} %fusion.4), channel_id=1, replica_groups=mesh['section'=8,'tp'=64] {'tp'}, dimensions={1} | all-to-all | bytes 4194304 | tf_op jit(solution)/shard_map/all_to_all | solution.py:101
  1238.8 2.9 copy.38
  1241.7 250.6 %all-gather.6.cloned.1.call-done = bf16[320,1,8192]{2,0,1:T(8,128)(2,1)} async-done(((bf16[320,1,128]{2,0,1:T(8,128)(2,1)}), bf16[320,1,8192]{2,0,1:T(8,128)(2,1)}) %all-gather.6.cloned.1.call-update) | async-done | bytes 5242896 | tf_op jit(solution)/shard_map/all_gather | solution.py:103
  1492.3 4.7 fusion.15
  1497.0 41.5 %collective-permute-start = (bf16[320,128]{1,0:T(8,128)(2,1)S(1)}, bf16[320,128]{1,0:T(8,128)(2,1)S(1)}, u32[]{:S(2)}, u32[]{:S(2)}) collective-permute-start(bf16[320,128]{1,0:T(8,128)(2,1)S(1)} %fusion.15), channel_id=1, source_target_pairs={{0,64},{64,128},{128,192},{192,256},{256,320},{320,384},{384,448},... | collective-permute-start | bytes 245768 | tf_op jit(solution)/shard_map/ppermute | solution.py:18
  (48 shorter events, 17.1 us)
Async XLA Ops:
  6.5 881.1 %all-reduce.2.cloned.1.call-start = ((), (), s32[]{:S(2)}) async-start(), calls=%async_computation.2 | async-start | bytes 5242880 | tf_op jit(solution)/shard_map/psum | solution.py:82
  175.7 0.9 copy-start.2
  175.8 1012.4 %all-gather.4.cloned.1.call-start = ((), (), s32[]{:S(2)}) async-start(), calls=%async_computation.3 | async-start | bytes 5324800 | tf_op jit(solution)/shard_map/all_gather | solution.py:75
  177.4 3.3 copy-start.4
  177.4 3.3 copy-start.5
  182.5 741.0 %all-to-all-start = ((bf16[128,64,128]{0,2,1:T(8,128)(2,1)}), bf16[128,64,128]{0,2,1:T(8,128)(2,1)}, u32[]{:S(2)}, u32[]{:S(2)}) async-start(bf16[128,64,128]{0,2,1:T(8,128)(2,1)} %fusion.5), calls=%async_computation | async-start | bytes 4194304 | tf_op jit(solution)/shard_map/all_to_all | solution.py:77
  188.1 1304.2 %all-gather.6.cloned.1.call-start = ((), (), s32[]{:S(2)}) async-start(), calls=%async_computation.4 | async-start | bytes 5324800 | tf_op jit(solution)/shard_map/all_gather | solution.py:103
  899.0 3.7 copy-start.1
  918.0 2.7 copy-start
  932.8 261.2 %copy-start.3 = (s32[320]{0:T(512)S(1)}, s32[320]{0:T(512)}, u32[]{:S(2)}) copy-start(s32[320]{0:T(512)} %param.23) | copy-start | bytes 3844
  1197.0 3.5 copy-start.6
  1197.0 3.5 copy-start.7
  1497.0 43.0 %collective-permute-start = (bf16[320,128]{1,0:T(8,128)(2,1)S(1)}, bf16[320,128]{1,0:T(8,128)(2,1)S(1)}, u32[]{:S(2)}, u32[]{:S(2)}) collective-permute-start(bf16[320,128]{1,0:T(8,128)(2,1)S(1)} %fusion.15), channel_id=1, source_target_pairs={{0,64},{64,128},{128,192},{192,256},{256,320},{320,384},{384,448},... | collective-permute-start | bytes 245768 | tf_op jit(solution)/shard_map/ppermute | solution.py:18
Sparse Core Ops, SparseCore 0:
  175.9 711.7 all-reduce.1
  889.7 298.4 all-gather.3
  1197.1 295.1 all-gather.5
where the time goes:
time: 1550 us
  waiting for transfers between devices  1210 us (78%)
  blocking collectives  201 us (13%)
  starting transfers between devices  47.2 us (3%)
  local copies, waits for them, and re-layouts  46.4 us (3%)
  other arithmetic  16 us (1%)
  matrix products  15.9 us (1%)
    psum x1, waiting for transfers between devices, local(): lax.psum(jnp.dot(normed, kv_eff, preferred_element_type=jnp.float32), 'tp')  699 us
    all_gather x1, waiting for transfers between devices, local(): normed_all = lax.all_gather(normed, 'tp', axis=1, tiled=True)  255 us
    all_gather x1, waiting for transfers between devices, local(): lax.all_gather(head_out, 'tp', axis=1, tiled=True)  251 us
    psum x1, blocking collectives, local(): squares = lax.psum(partial_value, 'tp')  164 us
    ppermute x1, starting transfers between devices, passed_along(): return lax.ppermute(value, axis, pairs)  41.5 us
    all_to_all x1, blocking collectives, local(): lax.all_to_all(o_eff, 'tp', split_axis=1, concat_axis=0, tiled=True)  37.8 us
  transfers between devices with their start and end apart: 5, of which 4 were waited for; matrix products, arithmetic and copies ran while one was open for 4% of the time, Pallas kernels for 0%

commit v1 on v0

--- a/solution.py
+++ b/solution.py
@@ -68,7 +68,7 @@
     kv_width = KV_HEADS * HD
     group_size = HEADS // KV_HEADS
     partial_value = jnp.sum(activ * activ, axis=1, keepdims=True)
-    squares = lax.psum(partial_value, "tp")
+    squares = jnp.sum(lax.all_gather(partial_value, "tp"), axis=0)
     normed = (activ * lax.rsqrt(squares / D + epsilon) * norm_gain[0].astype(jnp.float32)).astype(
         jnp.bfloat16
     )

time: 1550 us -> 2000 us (1.29)
  waiting for transfers between devices: 1210 us -> 1820 us
  blocking collectives: 201 us -> 37.8 us
    unnamed x3 -> x5, waiting for transfers between devices: 0.05 us -> 624 us
    psum x1 -> x0, blocking collectives: 164 us -> none  [local(): squares = lax.psum(partial_value, 'tp')]
  transfers between devices with their start and end apart: 5 -> 6, of which waited for: 4 -> 5; matrix products, arithmetic and copies ran while one was open for 4% -> 3% of each run, Pallas kernels for 0% -> 0%
where the time goes in v1:
time: 2000 us
  waiting for transfers between devices  1820 us (91%)
  local copies, waits for them, and re-layouts  49.6 us (2%)
  starting transfers between devices  49.2 us (2%)
  blocking collectives  37.8 us (2%)
    psum x1, waiting for transfers between devices, local(): lax.psum(jnp.dot(normed, kv_eff, preferred_element_type=jnp.float32), 'tp')  687 us
    unnamed x5, waiting for transfers between devices  624 us
    all_gather x1, waiting for transfers between devices, local(): normed_all = lax.all_gather(normed, 'tp', axis=1, tiled=True)  255 us
    all_gather x1, waiting for transfers between devices, local(): lax.all_gather(head_out, 'tp', axis=1, tiled=True)  251 us
    ppermute x1, starting transfers between devices, passed_along(): return lax.ppermute(value, axis, pairs)  41.5 us
  transfers between devices with their start and end apart: 6, of which 5 were waited for; matrix products, arithmetic and copies ran while one was open for 3% of the time, Pallas kernels for 0%

profile of v1, /device:TPU:1, one launch (start us, length us, event | category | flops | bytes accessed | tf_op | source)
XLA Modules:
  0.0 2000.1 jit_solution(5034334032522002702)
XLA Ops:
  11.9 623.5 %all-reduce.6.cloned.1.call-done = f32[20480]{0:T(1024)} async-done(((f32[20480]{0:T(1024)}), f32[20480]{0:T(1024)}) %all-reduce.6.cloned.1.call-update) | async-done | bytes 81936
  636.4 3.1 fusion.20
  641.2 3.2 copy.41
  646.4 7.5 all-to-all-start
  654.0 686.6 %all-reduce.4.cloned.1.call-done = f32[320,2048]{1,0:T(8,128)} async-done(((f32[320,2048]{1,0:T(8,128)}), f32[320,2048]{1,0:T(8,128)}) %all-reduce.4.cloned.1.call-update) | async-done | bytes 2621456 | tf_op jit(solution)/shard_map/psum | solution.py:82
  1340.7 3.5 copy.36
  1344.1 3.7 reshape.392
  1347.9 4.1 fusion.55
  1352.0 3.7 copy.48
  1355.7 3.4 copy.49
  1359.1 7.1 multiply_subtract_fusion
  1370.9 2.7 copy.40
  1373.6 2.8 select_convert_fusion
  1376.5 3.2 copy.42
  1379.7 3.0 copy.43
  1382.7 3.2 dot_general.21
  1385.9 255.4 %all-gather.5.cloned.1.call-done = bf16[320,8192]{1,0:T(8,128)(2,1)} async-done(((bf16[320,128]{1,0:T(8,128)(2,1)}), bf16[320,8192]{1,0:T(8,128)(2,1)}) %all-gather.5.cloned.1.call-update) | async-done | bytes 5242896 | tf_op jit(solution)/shard_map/all_gather | solution.py:75
  1641.2 5.1 fusion.2
  1650.0 3.4 copy.46
  1654.0 37.8 %all_to_all.32 = bf16[128,64,128]{0,2,1:T(8,128)(2,1)S(1)} all-to-all(bf16[128,64,128]{0,2,1:T(8,128)(2,1)S(1)} %fusion.4), channel_id=1, replica_groups=mesh['section'=8,'tp'=64] {'tp'}, dimensions={1} | all-to-all | bytes 4194304 | tf_op jit(solution)/shard_map/all_to_all | solution.py:101
  1691.8 2.9 copy.47
  1694.7 250.5 %all-gather.7.cloned.1.call-done = bf16[320,1,8192]{2,0,1:T(8,128)(2,1)} async-done(((bf16[320,1,128]{2,0,1:T(8,128)(2,1)}), bf16[320,1,8192]{2,0,1:T(8,128)(2,1)}) %all-gather.7.cloned.1.call-update) | async-done | bytes 5242896 | tf_op jit(solution)/shard_map/all_gather | solution.py:103
  1945.2 4.7 fusion.15
  1949.9 41.5 %collective-permute-start = (bf16[320,128]{1,0:T(8,128)(2,1)S(1)}, bf16[320,128]{1,0:T(8,128)(2,1)S(1)}, u32[]{:S(2)}, u32[]{:S(2)}) collective-permute-start(bf16[320,128]{1,0:T(8,128)(2,1)S(1)} %fusion.15), channel_id=1, source_target_pairs={{0,64},{64,128},{128,192},{192,256},{256,320},{320,384},{384,448},... | collective-permute-start | bytes 245768 | tf_op jit(solution)/shard_map/ppermute | solution.py:18
  (56 shorter events, 20.3 us)
Async XLA Ops:
  6.5 628.9 %all-reduce.6.cloned.1.call-start = ((), (), s32[]{:S(2)}) async-start(), calls=%async_computation.5 | async-start | bytes 163840
  9.8 0.6 copy-start.3
  10.4 1330.2 %all-reduce.4.cloned.1.call-start = ((), (), s32[]{:S(2)}) async-start(), calls=%async_computation.2 | async-start | bytes 5242880 | tf_op jit(solution)/shard_map/psum | solution.py:82
  639.6 0.9 copy-start.2
  639.6 1001.6 %all-gather.5.cloned.1.call-start = ((), (), s32[]{:S(2)}) async-start(), calls=%async_computation.3 | async-start | bytes 5324800 | tf_op jit(solution)/shard_map/all_gather | solution.py:75
  641.2 3.3 copy-start.5
  641.2 3.3 copy-start.6
  646.4 730.1 %all-to-all-start = ((bf16[128,64,128]{0,2,1:T(8,128)(2,1)}), bf16[128,64,128]{0,2,1:T(8,128)(2,1)}, u32[]{:S(2)}, u32[]{:S(2)}) async-start(bf16[128,64,128]{0,2,1:T(8,128)(2,1)} %fusion.5), calls=%async_computation | async-start | bytes 4194304 | tf_op jit(solution)/shard_map/all_to_all | solution.py:77
  653.9 1291.3 %all-gather.7.cloned.1.call-start = ((), (), s32[]{:S(2)}) async-start(), calls=%async_computation.4 | async-start | bytes 5324800 | tf_op jit(solution)/shard_map/all_gather | solution.py:103
  1352.0 3.7 copy-start.1
  1370.9 2.7 copy-start
  1385.8 261.2 %copy-start.4 = (s32[320]{0:T(512)S(1)}, s32[320]{0:T(512)}, u32[]{:S(2)}) copy-start(s32[320]{0:T(512)} %param.23) | copy-start | bytes 3844
  1650.0 3.5 copy-start.7
  1650.0 3.5 copy-start.8
  1949.9 43.0 %collective-permute-start = (bf16[320,128]{1,0:T(8,128)(2,1)S(1)}, bf16[320,128]{1,0:T(8,128)(2,1)S(1)}, u32[]{:S(2)}, u32[]{:S(2)}) collective-permute-start(bf16[320,128]{1,0:T(8,128)(2,1)S(1)} %fusion.15), channel_id=1, source_target_pairs={{0,64},{64,128},{128,192},{192,256},{256,320},{320,384},{384,448},... | collective-permute-start | bytes 245768 | tf_op jit(solution)/shard_map/ppermute | solution.py:18
Sparse Core Ops, SparseCore 0:
  10.6 624.7 all-reduce.5
  639.7 700.9 all-reduce.3
  1342.7 298.4 all-gather.4
  1650.1 295.0 all-gather.6
